TPU v7x, 32 devices: a whole 2x2x4 slice. The times are simulated.
32 devices in a mesh: mol: 2 (over x), occ: 16 (over z, y, core).
Axes of the slice: x: 2, y: 2, z: 4, core: 2. Of those that a mesh axis runs over, the one named last changes fastest.
Arguments:
- integrals: bfloat16 [512, 128, 2048], P(('mol', 'occ')), parts along dimension 0, may hold values from -6 to 6
- orbitals: bfloat16 [4096, 1536], P('mol'), parts along dimension 0
- occ_energy: float32 [256], P('mol'), parts along dimension 0, may hold values from -2 to -0.3
- vir_energy: float32 [3072], P('mol'), parts along dimension 0, may hold values from 0.1 to 3
- owner: int32 [16], P('mol'), parts along dimension 0, may hold values from 0 to 127
- vblock: int32 [16], P('mol'), parts along dimension 0, may hold values from 0 to 7
Outputs:
- factors: bfloat16 [512, 128, 1536], P('mol', 'occ'), parts along dimension 0
- pair_energy: float32 [256, 8], P(('mol', 'occ')), parts along dimension 0
There are 2 independent parts, one for each index of `mol`. A program takes and returns all parts, laid end to end along the dimension named above; each array names one. Nothing has to cross between parts.
Inputs may be any that keep to these rules, and one draw needn't show every extreme that they name: `owner`: each step names one occupied orbital and one virtual block; steps may repeat.
All inputs are finite; a program needn't handle non-finite values.
Results may differ from a plain program's by a relative error of at most 0.001.
Values may be sent and summed in bfloat16 or wider, within the bound.
No kernel may reach another device: no remote copies, remote signals or barrier semaphores. Data moves between devices by JAX's collectives and lax.ppermute only.
A program may use at most 128 MiB of HBM per device.

v0:
```python
import jax
import jax.numpy as jnp
from jax import lax
from jax.sharding import PartitionSpec as P

VBLK = 192


def pair_column(factors, block, occ_here, occ_energy, vir_energy, orbital_j, block_id):
    coulomb = lax.dot_general(
        factors, block, (((0,), (0,)), ((), ())), preferred_element_type=jnp.float32
    )
    vir_block = lax.dynamic_slice(vir_energy, (block_id * VBLK,), (VBLK,))
    occ_j = occ_energy[orbital_j]
    denom = vir_energy[None, :, None] + vir_block[None, None, :] - occ_here[:, None, None] - occ_j
    scale = 1.0 / (factors.shape[0] * vir_energy.shape[0] * VBLK)
    return -jnp.sum(coulomb * coulomb / denom, axis=(1, 2)) * scale


def per_device(integrals, orbitals, occ_energy, vir_energy, owner, vblock):
    aux_here, occ_total, basis_count = integrals.shape
    step_count = owner.shape[0]
    flat = integrals.reshape(aux_here * occ_total, basis_count)
    product = jnp.dot(flat, orbitals, preferred_element_type=jnp.float32).astype(jnp.bfloat16)
    product = product.reshape(aux_here, occ_total, orbitals.shape[1])

    def own_piece(step):
        piece = lax.dynamic_slice(
            product, (jnp.int32(0), owner[step], vblock[step] * VBLK), (aux_here, 1, VBLK)
        )
        return piece[:, 0, :]

    pieces = jnp.stack([own_piece(step) for step in range(step_count)], axis=1)
    blocks = lax.all_gather(pieces, "occ", axis=0, tiled=True)
    factors = lax.all_to_all(product, "occ", split_axis=1, concat_axis=0, tiled=True)
    local_count = factors.shape[1]
    occ_here = lax.dynamic_slice(occ_energy, (lax.axis_index("occ") * local_count,), (local_count,))
    energies = jnp.zeros((local_count, step_count), jnp.float32)

    def step_body(step, energies):
        orbital_j = owner[step]
        block_id = vblock[step]
        block = lax.dynamic_index_in_dim(blocks, step, axis=1, keepdims=False)
        column = pair_column(factors, block, occ_here, occ_energy, vir_energy, orbital_j, block_id)
        return lax.dynamic_update_slice(energies, column[:, None], (jnp.int32(0), step))

    energies = lax.fori_loop(0, step_count, step_body, energies)
    return (factors, energies)


def solution(mesh):
    placed = (P(("mol", "occ"), None, None), P("mol", None), P("mol"), P("mol"), P("mol"), P("mol"))
    return jax.shard_map(
        per_device,
        mesh=mesh,
        in_specs=placed,
        out_specs=(P("mol", "occ", None), P(("mol", "occ"), None)),
        check_vma=False,
    )
```

profile of v0, /device:TPU:9, one launch (start us, length us, event | category | flops | bytes accessed | tf_op | source)
XLA Modules:
  0.0 285.7 jit_solution(6650717841820332586)
XLA Ops:
  0.6 17.3 %convolution_convert_fusion = bf16[2048,1536]{1,0:T(8,128)(2,1)S(1)} fusion(bf16[2048,2048]{1,0:T(8,128)(2,1)} %bitcast.56, bf16[2048,1536]{1,0:T(8,128)(2,1)} %param.9), kind=kOutput, calls=%fused_computation.7 | convolution fusion | flops 12888047616 | bytes 20971520 | tf_op jit(solution)/shard_map/dot_general | solution.py:24
  17.9 2.6 copy-done.1
  20.5 6.2 %copy.19 = bf16[16,128,1536]{2,0,1:T(8,128)(2,1)} copy(bf16[16,128,1536]{2,1,0:T(8,128)(2,1)S(1)} %bitcast.54) | data formatting | bytes 12582912 | tf_op jit(solution)/shard_map/reshape | solution.py:25
  26.8 6.7 %all-to-all-start = ((bf16[16,128,1536]{2,0,1:T(8,128)(2,1)}), bf16[16,128,1536]{2,0,1:T(8,128)(2,1)}, u32[]{:S(2)}, u32[]{:S(2)}) async-start(bf16[16,128,1536]{2,0,1:T(8,128)(2,1)} %copy.19), calls=%async_computation | async-start | bytes 12582912 | tf_op jit(solution)/shard_map/all_to_all | solution.py:35
  33.5 0.7 fusion.4
  39.2 0.7 fusion.5
  55.2 1.5 constant_dynamic-slice_fusion
  57.0 127.9 %all_gather.3 = bf16[256,8,192]{2,1,0:T(8,128)(2,1)S(1)} all-gather(bf16[16,8,192]{2,1,0:T(8,128)(2,1)S(1)} %stack.3), channel_id=1, replica_groups=mesh['mol'=2,'occ'=16] {'occ'}, dimensions={0}, use_global_device_ids=true | all-gather | bytes 835584 | tf_op jit(solution)/shard_map/all_gather | solution.py:34
  184.8 1.0 copy.21
  185.9 6.9 %copy.20 = bf16[16,16,8,1536]{3,2,1,0:T(8,128)(2,1)S(1)} copy(bf16[16,16,8,1536]{3,1,2,0:T(8,128)(2,1)} %bitcast.10) | data formatting | bytes 12582912 | tf_op jit(solution)/shard_map/all_to_all | solution.py:35
  192.9 4.7 %copy.22 = bf16[256,8,1536]{2,0,1:T(8,128)(2,1)} copy(bf16[256,8,1536]{2,1,0:T(8,128)(2,1)S(1)} %bitcast.52) | data formatting | bytes 12582912 | tf_op jit(solution)/shard_map/while | solution.py:47
  197.6 87.4 %while.13 = (s32[]{:T(128)}, f32[8,8]{0,1:T(8,128)S(1)}, bf16[256,8,192]{0,2,1:T(8,128)(2,1)S(1)}, bf16[256,8,1536]{2,0,1:T(8,128)(2,1)}, f32[1536]{0:T(1024)S(1...) while((s32[]{:T(128)}, f32[8,8]{0,1:T(8,128)S(1)}, ...), condition=%wide.region_2.3_spmd, body=%wide.region_0.2_spmd.sunk | while | flops 1220050944 | bytes 8758441 | solution.py:47
  199.1 0.6 dynamic_slice.90
  202.2 6.3 %fusion.14 = f32[8]{0:T(128)S(1)} fusion(bf16[256,8,1536]{2,0,1:T(8,128)(2,1)} %get-tuple-element.307, f32[]{:T(128)} %bitcast.50, f32[8]{0:T(128)S(1)} %get-tuple-element.310, f32[1536,192]{0,1:T(8,128)S(1)} %broadcast_add_fusion.2, bf16[256,8,192]{0,2,1:T(8,128)(2,1)S(1)} %get-tuple-element.306, s32[]{:T(128)} %get-tuple-element.290), kind=kOutput, calls=%fused_computation.1.clone.1 | convolution fusion | flops 1219756032 | bytes 7569960 | tf_op jit(solution)/shard_map/while/body/eval_jaxpr/dot_general | solution.py:10
  210.0 0.6 dynamic_slice.90
  213.1 6.3 %fusion.14 = f32[8]{0:T(128)S(1)} fusion(bf16[256,8,1536]{2,0,1:T(8,128)(2,1)} %get-tuple-element.307, f32[]{:T(128)} %bitcast.50, f32[8]{0:T(128)S(1)} %get-tuple-element.310, f32[1536,192]{0,1:T(8,128)S(1)} %broadcast_add_fusion.2, bf16[256,8,192]{0,2,1:T(8,128)(2,1)S(1)} %get-tuple-element.306, s32[]{:T(128)} %get-tuple-element.290), kind=kOutput, calls=%fused_computation.1.clone.1 | convolution fusion | flops 1219756032 | bytes 7569960 | tf_op jit(solution)/shard_map/while/body/eval_jaxpr/dot_general | solution.py:10
  224.1 6.3 %fusion.14 = f32[8]{0:T(128)S(1)} fusion(bf16[256,8,1536]{2,0,1:T(8,128)(2,1)} %get-tuple-element.307, f32[]{:T(128)} %bitcast.50, f32[8]{0:T(128)S(1)} %get-tuple-element.310, f32[1536,192]{0,1:T(8,128)S(1)} %broadcast_add_fusion.2, bf16[256,8,192]{0,2,1:T(8,128)(2,1)S(1)} %get-tuple-element.306, s32[]{:T(128)} %get-tuple-element.290), kind=kOutput, calls=%fused_computation.1.clone.1 | convolution fusion | flops 1219756032 | bytes 7569960 | tf_op jit(solution)/shard_map/while/body/eval_jaxpr/dot_general | solution.py:10
  235.0 6.3 %fusion.14 = f32[8]{0:T(128)S(1)} fusion(bf16[256,8,1536]{2,0,1:T(8,128)(2,1)} %get-tuple-element.307, f32[]{:T(128)} %bitcast.50, f32[8]{0:T(128)S(1)} %get-tuple-element.310, f32[1536,192]{0,1:T(8,128)S(1)} %broadcast_add_fusion.2, bf16[256,8,192]{0,2,1:T(8,128)(2,1)S(1)} %get-tuple-element.306, s32[]{:T(128)} %get-tuple-element.290), kind=kOutput, calls=%fused_computation.1.clone.1 | convolution fusion | flops 1219756032 | bytes 7569960 | tf_op jit(solution)/shard_map/while/body/eval_jaxpr/dot_general | solution.py:10
  245.9 6.3 %fusion.14 = f32[8]{0:T(128)S(1)} fusion(bf16[256,8,1536]{2,0,1:T(8,128)(2,1)} %get-tuple-element.307, f32[]{:T(128)} %bitcast.50, f32[8]{0:T(128)S(1)} %get-tuple-element.310, f32[1536,192]{0,1:T(8,128)S(1)} %broadcast_add_fusion.2, bf16[256,8,192]{0,2,1:T(8,128)(2,1)S(1)} %get-tuple-element.306, s32[]{:T(128)} %get-tuple-element.290), kind=kOutput, calls=%fused_computation.1.clone.1 | convolution fusion | flops 1219756032 | bytes 7569960 | tf_op jit(solution)/shard_map/while/body/eval_jaxpr/dot_general | solution.py:10
  256.9 6.3 %fusion.14 = f32[8]{0:T(128)S(1)} fusion(bf16[256,8,1536]{2,0,1:T(8,128)(2,1)} %get-tuple-element.307, f32[]{:T(128)} %bitcast.50, f32[8]{0:T(128)S(1)} %get-tuple-element.310, f32[1536,192]{0,1:T(8,128)S(1)} %broadcast_add_fusion.2, bf16[256,8,192]{0,2,1:T(8,128)(2,1)S(1)} %get-tuple-element.306, s32[]{:T(128)} %get-tuple-element.290), kind=kOutput, calls=%fused_computation.1.clone.1 | convolution fusion | flops 1219756032 | bytes 7569960 | tf_op jit(solution)/shard_map/while/body/eval_jaxpr/dot_general | solution.py:10
  264.7 0.6 dynamic_slice.90
  267.8 6.3 %fusion.14 = f32[8]{0:T(128)S(1)} fusion(bf16[256,8,1536]{2,0,1:T(8,128)(2,1)} %get-tuple-element.307, f32[]{:T(128)} %bitcast.50, f32[8]{0:T(128)S(1)} %get-tuple-element.310, f32[1536,192]{0,1:T(8,128)S(1)} %broadcast_add_fusion.2, bf16[256,8,192]{0,2,1:T(8,128)(2,1)S(1)} %get-tuple-element.306, s32[]{:T(128)} %get-tuple-element.290), kind=kOutput, calls=%fused_computation.1.clone.1 | convolution fusion | flops 1219756032 | bytes 7569960 | tf_op jit(solution)/shard_map/while/body/eval_jaxpr/dot_general | solution.py:10
  278.7 6.3 %fusion.14 = f32[8]{0:T(128)S(1)} fusion(bf16[256,8,1536]{2,0,1:T(8,128)(2,1)} %get-tuple-element.307, f32[]{:T(128)} %bitcast.50, f32[8]{0:T(128)S(1)} %get-tuple-element.310, f32[1536,192]{0,1:T(8,128)S(1)} %broadcast_add_fusion.2, bf16[256,8,192]{0,2,1:T(8,128)(2,1)S(1)} %get-tuple-element.306, s32[]{:T(128)} %get-tuple-element.290), kind=kOutput, calls=%fused_computation.1.clone.1 | convolution fusion | flops 1219756032 | bytes 7569960 | tf_op jit(solution)/shard_map/while/body/eval_jaxpr/dot_general | solution.py:10
  285.0 0.7 copy.23
  (68 shorter events, 15.2 us)
Async XLA Ops:
  17.9 2.6 copy-start.1
  26.7 6.8 %copy-start.4 = (s32[8]{0:T(128)S(1)}, s32[8]{0:T(128)}, u32[]{:S(2)}) copy-start(s32[8]{0:T(128)} %param.13) | copy-start | bytes 100
  26.7 12.5 %copy-start.3 = (s32[8]{0:T(128)S(1)}, s32[8]{0:T(128)}, u32[]{:S(2)}) copy-start(s32[8]{0:T(128)} %param.12) | copy-start | bytes 100
  26.7 159.1 %copy-start.5 = (f32[128]{0:T(128)S(1)}, f32[128]{0:T(128)}, u32[]{:S(2)}) copy-start(f32[128]{0:T(128)} %param.10) | copy-start | bytes 1540
  26.8 159.2 %all-to-all-start = ((bf16[16,128,1536]{2,0,1:T(8,128)(2,1)}), bf16[16,128,1536]{2,0,1:T(8,128)(2,1)}, u32[]{:S(2)}, u32[]{:S(2)}) async-start(bf16[16,128,1536]{2,0,1:T(8,128)(2,1)} %copy.19), calls=%async_computation | async-start | bytes 12582912 | tf_op jit(solution)/shard_map/all_to_all | solution.py:35
  192.8 4.7 %copy-start = (bf16[16,16,8,1536]{3,2,1,0:T(8,128)(2,1)}, bf16[16,16,8,1536]{3,2,1,0:T(8,128)(2,1)S(1)}, u32[]{:S(2)}) copy-start(bf16[16,16,8,1536]{3,2,1,0:T(8,128)(2,1)S(1)} %copy.20) | copy-start | bytes 18874372
  192.8 4.7 %copy-start.2 = (f32[1536]{0:T(1024)S(1)}, f32[1536]{0:T(1024)}, u32[]{:S(2)}) copy-start(f32[1536]{0:T(1024)} %param.11) | copy-start | bytes 18436
where the time goes:
time: 287 us; the launch traced here: 286 us
  blocking collectives  128 us (45%)
  matrix products  67.4 us (23%)
  local copies, waits for them, and re-layouts  40.8 us (14%)
  between operations  21.1 us (7%)
  loops' own time  20.6 us (7%)
  starting transfers between devices  6.74 us (2%)
    all_gather x1, blocking collectives, per_device(): blocks = lax.all_gather(pieces, 'occ', axis=0, tiled=True)  128 us
    dot_general x8, matrix products, pair_column(): lax.dot_general(factors, block, (((0,), (0,)), ((), ())), preferred_eleme...  50.1 us
    another operation x1, loops' own time, per_device(): energies = lax.fori_loop(0, step_count, step_body, energies)  20.6 us
    dot_general x1, matrix products, per_device(): jnp.dot(flat, orbitals, preferred_element_type=jnp.float32)  17.3 us
    all_to_all x1, local copies, waits for them, and re-layouts, per_device(): lax.all_to_all(product, 'occ', split_axis=1, concat_axis=0, tiled=True)  6.9 us
    all_to_all x1, starting transfers between devices, per_device(): lax.all_to_all(product, 'occ', split_axis=1, concat_axis=0, tiled=True)  6.74 us
    reshape x1, local copies, waits for them, and re-layouts, per_device(): product = product.reshape(aux_here, occ_total, orbitals.shape[1])  6.2 us
  transfers between devices with their start and end apart: 1, of which 0 were waited for; matrix products, arithmetic and copies ran while one was open for 1% of the time, Pallas kernels for 0%

commit v1 on v0

--- a/solution.py
+++ b/solution.py
@@ -32,7 +32,10 @@
 
     pieces = jnp.stack([own_piece(step) for step in range(step_count)], axis=1)
     blocks = lax.all_gather(pieces, "occ", axis=0, tiled=True)
-    factors = lax.all_to_all(product, "occ", split_axis=1, concat_axis=0, tiled=True)
+    factors = jnp.concatenate(
+        lax.all_to_all(jnp.stack(jnp.split(product, lax.axis_size("occ"), axis=1)), "occ", 0, 0),
+        axis=0,
+    )
     local_count = factors.shape[1]
     occ_here = lax.dynamic_slice(occ_energy, (lax.axis_index("occ") * local_count,), (local_count,))
     energies = jnp.zeros((local_count, step_count), jnp.float32)

time: 287 us -> 292 us (1.017)
  local copies, waits for them, and re-layouts: 40.8 us -> 46.5 us
    unnamed x13 -> x27, local copies, waits for them, and re-layouts: 3.32 us -> 18.9 us
    all_to_all x1 -> x0, local copies, waits for them, and re-layouts: 6.9 us -> none  [per_device(): lax.all_to_all(product, 'occ', split_axis=1, concat_axis=0, tiled=True)]
    reshape x1 -> x0, local copies, waits for them, and re-layouts: 6.2 us -> none  [per_device(): product = product.reshape(aux_here, occ_total, orbitals.shape[1])]
where the time goes in v1:
time: 292 us; the launch traced here: 291 us
  blocking collectives  128 us (44%)
  matrix products  67.3 us (23%)
  local copies, waits for them, and re-layouts  46.5 us (16%)
  between operations  21.1 us (7%)
  loops' own time  20.1 us (7%)
  starting transfers between devices  6.74 us (2%)
    all_gather x1, blocking collectives, per_device(): blocks = lax.all_gather(pieces, 'occ', axis=0, tiled=True)  128 us
    dot_general x8, matrix products, pair_column(): lax.dot_general(factors, block, (((0,), (0,)), ((), ())), preferred_eleme...  50 us
    another operation x1, loops' own time, per_device(): energies = lax.fori_loop(0, step_count, step_body, energies)  20.1 us
    unnamed x27, local copies, waits for them, and re-layouts  18.9 us
    dot_general x1, matrix products, per_device(): jnp.dot(flat, orbitals, preferred_element_type=jnp.float32)  17.3 us
    while x2, local copies, waits for them, and re-layouts, per_device(): energies = lax.fori_loop(0, step_count, step_body, energies)  8.51 us
    all_to_all x1, starting transfers between devices, per_device(): lax.all_to_all(jnp.stack(jnp.split(product, lax.axis_size('occ'), axis=1)...  6.74 us
  transfers between devices with their start and end apart: 1, of which 0 were waited for; matrix products, arithmetic and copies ran while one was open for 1% of the time, Pallas kernels for 0%

profile of v1, /device:TPU:9, one launch (start us, length us, event | category | flops | bytes accessed | tf_op | source)
XLA Modules:
  0.0 290.7 jit_solution(9168520508391145790)
XLA Ops:
  0.6 17.3 %convolution_convert_fusion = bf16[2048,1536]{1,0:T(8,128)(2,1)S(1)} fusion(bf16[2048,2048]{1,0:T(8,128)(2,1)} %bitcast.130, bf16[2048,1536]{1,0:T(8,128)(2,1)} %param.9), kind=kOutput, calls=%fused_computation.7 | convolution fusion | flops 12888047616 | bytes 20971520 | tf_op jit(solution)/shard_map/dot_general | solution.py:24
  17.9 0.8 fusion.19
  18.8 1.3 fusion.18
  20.1 0.9 fusion.17
  21.0 0.8 fusion.16
  24.0 0.8 fusion.12
  26.4 0.8 fusion.9
  28.7 0.8 fusion.6
  30.2 0.8 fusion.4
  31.0 6.7 %all-to-all-start = ((bf16[16,16,8,1536]{3,2,1,0:T(8,128)(2,1)}), bf16[16,16,8,1536]{3,2,1,0:T(8,128)(2,1)}, u32[]{:S(2)}, u32[]{:S(2)}) async-start(bf16[16,16,8,1536]{3,2,1,0:T(8,128)(2,1)} %fusion.4), calls=%async_computation | async-start | bytes 12582912 | tf_op jit(solution)/shard_map/all_to_all | solution.py:36
  59.6 1.5 constant_dynamic-slice_fusion
  61.3 127.8 %all_gather.3 = bf16[256,8,192]{2,1,0:T(8,128)(2,1)S(1)} all-gather(bf16[16,8,192]{2,1,0:T(8,128)(2,1)S(1)} %stack.71), channel_id=1, replica_groups=mesh['mol'=2,'occ'=16] {'occ'}, dimensions={0}, use_global_device_ids=true | all-gather | bytes 835584 | tf_op jit(solution)/shard_map/all_gather | solution.py:34
  189.1 1.0 copy.18
  190.2 7.5 %copy.19 = bf16[256,8,1536]{2,0,1:T(8,128)(2,1)} copy(bf16[256,8,1536]{2,1,0:T(8,128)(2,1)} %bitcast.25) | data formatting | bytes 12582912 | tf_op jit(solution)/shard_map/while | solution.py:50
  197.7 86.4 %while.13 = (s32[]{:T(128)}, f32[8,8]{0,1:T(8,128)S(1)}, bf16[256,8,192]{0,2,1:T(8,128)(2,1)S(1)}, bf16[256,8,1536]{2,0,1:T(8,128)(2,1)}, f32[1536]{0:T(1024)S(1...) while((s32[]{:T(128)}, f32[8,8]{0,1:T(8,128)S(1)}, ...), condition=%wide.region_2.3_spmd, body=%wide.region_0.2_spmd.sunk | while | flops 1220050944 | bytes 8758441 | solution.py:50
  202.2 6.2 %fusion.30 = f32[8]{0:T(128)S(1)} fusion(bf16[256,8,1536]{2,0,1:T(8,128)(2,1)} %get-tuple-element.307, f32[]{:T(128)} %bitcast.111, f32[8]{0:T(128)S(1)} %get-tuple-element.310, f32[1536,192]{0,1:T(8,128)S(1)} %broadcast_add_fusion.2, bf16[256,8,192]{0,2,1:T(8,128)(2,1)S(1)} %get-tuple-element.306, s32[]{:T(128)} %get-tuple-element.290), kind=kOutput, calls=%fused_computation.1.clone.1 | convolution fusion | flops 1219756032 | bytes 7569960 | tf_op jit(solution)/shard_map/while/body/eval_jaxpr/dot_general | solution.py:10
  213.0 6.2 %fusion.30 = f32[8]{0:T(128)S(1)} fusion(bf16[256,8,1536]{2,0,1:T(8,128)(2,1)} %get-tuple-element.307, f32[]{:T(128)} %bitcast.111, f32[8]{0:T(128)S(1)} %get-tuple-element.310, f32[1536,192]{0,1:T(8,128)S(1)} %broadcast_add_fusion.2, bf16[256,8,192]{0,2,1:T(8,128)(2,1)S(1)} %get-tuple-element.306, s32[]{:T(128)} %get-tuple-element.290), kind=kOutput, calls=%fused_computation.1.clone.1 | convolution fusion | flops 1219756032 | bytes 7569960 | tf_op jit(solution)/shard_map/while/body/eval_jaxpr/dot_general | solution.py:10
  223.8 6.2 %fusion.30 = f32[8]{0:T(128)S(1)} fusion(bf16[256,8,1536]{2,0,1:T(8,128)(2,1)} %get-tuple-element.307, f32[]{:T(128)} %bitcast.111, f32[8]{0:T(128)S(1)} %get-tuple-element.310, f32[1536,192]{0,1:T(8,128)S(1)} %broadcast_add_fusion.2, bf16[256,8,192]{0,2,1:T(8,128)(2,1)S(1)} %get-tuple-element.306, s32[]{:T(128)} %get-tuple-element.290), kind=kOutput, calls=%fused_computation.1.clone.1 | convolution fusion | flops 1219756032 | bytes 7569960 | tf_op jit(solution)/shard_map/while/body/eval_jaxpr/dot_general | solution.py:10
  234.6 6.2 %fusion.30 = f32[8]{0:T(128)S(1)} fusion(bf16[256,8,1536]{2,0,1:T(8,128)(2,1)} %get-tuple-element.307, f32[]{:T(128)} %bitcast.111, f32[8]{0:T(128)S(1)} %get-tuple-element.310, f32[1536,192]{0,1:T(8,128)S(1)} %broadcast_add_fusion.2, bf16[256,8,192]{0,2,1:T(8,128)(2,1)S(1)} %get-tuple-element.306, s32[]{:T(128)} %get-tuple-element.290), kind=kOutput, calls=%fused_computation.1.clone.1 | convolution fusion | flops 1219756032 | bytes 7569960 | tf_op jit(solution)/shard_map/while/body/eval_jaxpr/dot_general | solution.py:10
  245.4 6.2 %fusion.30 = f32[8]{0:T(128)S(1)} fusion(bf16[256,8,1536]{2,0,1:T(8,128)(2,1)} %get-tuple-element.307, f32[]{:T(128)} %bitcast.111, f32[8]{0:T(128)S(1)} %get-tuple-element.310, f32[1536,192]{0,1:T(8,128)S(1)} %broadcast_add_fusion.2, bf16[256,8,192]{0,2,1:T(8,128)(2,1)S(1)} %get-tuple-element.306, s32[]{:T(128)} %get-tuple-element.290), kind=kOutput, calls=%fused_computation.1.clone.1 | convolution fusion | flops 1219756032 | bytes 7569960 | tf_op jit(solution)/shard_map/while/body/eval_jaxpr/dot_general | solution.py:10
  256.2 6.2 %fusion.30 = f32[8]{0:T(128)S(1)} fusion(bf16[256,8,1536]{2,0,1:T(8,128)(2,1)} %get-tuple-element.307, f32[]{:T(128)} %bitcast.111, f32[8]{0:T(128)S(1)} %get-tuple-element.310, f32[1536,192]{0,1:T(8,128)S(1)} %broadcast_add_fusion.2, bf16[256,8,192]{0,2,1:T(8,128)(2,1)S(1)} %get-tuple-element.306, s32[]{:T(128)} %get-tuple-element.290), kind=kOutput, calls=%fused_computation.1.clone.1 | convolution fusion | flops 1219756032 | bytes 7569960 | tf_op jit(solution)/shard_map/while/body/eval_jaxpr/dot_general | solution.py:10
  267.0 6.2 %fusion.30 = f32[8]{0:T(128)S(1)} fusion(bf16[256,8,1536]{2,0,1:T(8,128)(2,1)} %get-tuple-element.307, f32[]{:T(128)} %bitcast.111, f32[8]{0:T(128)S(1)} %get-tuple-element.310, f32[1536,192]{0,1:T(8,128)S(1)} %broadcast_add_fusion.2, bf16[256,8,192]{0,2,1:T(8,128)(2,1)S(1)} %get-tuple-element.306, s32[]{:T(128)} %get-tuple-element.290), kind=kOutput, calls=%fused_computation.1.clone.1 | convolution fusion | flops 1219756032 | bytes 7569960 | tf_op jit(solution)/shard_map/while/body/eval_jaxpr/dot_general | solution.py:10
  277.9 6.2 %fusion.30 = f32[8]{0:T(128)S(1)} fusion(bf16[256,8,1536]{2,0,1:T(8,128)(2,1)} %get-tuple-element.307, f32[]{:T(128)} %bitcast.111, f32[8]{0:T(128)S(1)} %get-tuple-element.310, f32[1536,192]{0,1:T(8,128)S(1)} %broadcast_add_fusion.2, bf16[256,8,192]{0,2,1:T(8,128)(2,1)S(1)} %get-tuple-element.306, s32[]{:T(128)} %get-tuple-element.290), kind=kOutput, calls=%fused_computation.1.clone.1 | convolution fusion | flops 1219756032 | bytes 7569960 | tf_op jit(solution)/shard_map/while/body/eval_jaxpr/dot_general | solution.py:10
  284.8 5.9 %copy.44 = bf16[256,8,1536]{2,1,0:T(8,128)(2,1)} copy(bf16[256,8,1536]{2,1,0:T(8,128)(2,1)} %bitcast.25) | data formatting | bytes 12582912
  (81 shorter events, 24.9 us)
Async XLA Ops:
  17.9 12.3 %copy-start = (bf16[2048,1536]{1,0:T(8,128)(2,1)}, bf16[2048,1536]{1,0:T(8,128)(2,1)S(1)}, u32[]{:S(2)}) copy-start(bf16[2048,1536]{1,0:T(8,128)(2,1)S(1)} %convolution_convert_fusion) | copy-start | bytes 18874372
  31.0 6.8 %copy-start.3 = (s32[8]{0:T(128)S(1)}, s32[8]{0:T(128)}, u32[]{:S(2)}) copy-start(s32[8]{0:T(128)} %param.13) | copy-start | bytes 100
  31.0 12.5 %copy-start.2 = (s32[8]{0:T(128)S(1)}, s32[8]{0:T(128)}, u32[]{:S(2)}) copy-start(s32[8]{0:T(128)} %param.12) | copy-start | bytes 100
  31.0 159.1 %copy-start.4 = (f32[128]{0:T(128)S(1)}, f32[128]{0:T(128)}, u32[]{:S(2)}) copy-start(f32[128]{0:T(128)} %param.10) | copy-start | bytes 1540
  31.0 159.2 %all-to-all-start = ((bf16[16,16,8,1536]{3,2,1,0:T(8,128)(2,1)}), bf16[16,16,8,1536]{3,2,1,0:T(8,128)(2,1)}, u32[]{:S(2)}, u32[]{:S(2)}) async-start(bf16[16,16,8,1536]{3,2,1,0:T(8,128)(2,1)} %fusion.4), calls=%async_computation | async-start | bytes 12582912 | tf_op jit(solution)/shard_map/all_to_all | solution.py:36
  190.2 7.5 %copy-start.1 = (f32[1536]{0:T(1024)S(1)}, f32[1536]{0:T(1024)}, u32[]{:S(2)}) copy-start(f32[1536]{0:T(1024)} %param.11) | copy-start | bytes 18436
